TPU v7x, 256 devices: a whole 4x4x8 slice. The times are simulated.
256 devices in a mesh: dp: 32 (over y, x, core), tensor: 8 (over z).
Axes of the slice: x: 4, y: 4, z: 8, core: 2. Of those that a mesh axis runs over, the one named last changes fastest.
Arguments:
- tokens: bfloat16 [8192, 8192], P('dp'), may hold values from -6 to 6
- router_weight: bfloat16 [8192, 32], replicated, may hold values from -0.0625 to 0.0625
- gate_weight: bfloat16 [14336, 8192], P(('dp', 'tensor')), may hold values from -0.0625 to 0.0625
- up_weight: bfloat16 [14336, 8192], P(('dp', 'tensor')), may hold values from -0.0625 to 0.0625
- down_weight: bfloat16 [14336, 8192], P(('dp', 'tensor')), may hold values from -0.25 to 0.25
- cluster_of: int32 [14336, 1], P('dp'), may hold values from 0 to 31; in each aligned block of 448 rows (0 to 447, 448 to 895, ...) at most 28 rows name the same one
- expert_ids: int32 [8192, 2], P('dp'), may hold values from 0 to 31, all different within a row; in each aligned block of 256 rows (0 to 255, 256 to 511, ...) at most 32 rows name the same one
Outputs:
- mixed_out: bfloat16 [8192, 8192], P('dp', 'tensor')
Inputs may be any that keep to these rules, and one draw needn't show every extreme that they name: `expert_ids`: in each aligned block of 256 rows (the tokens of one dp index) no expert is named by more than 32 rows, a bound that some block reaches; a row names two different experts; every expert is named somewhere. `cluster_of`: in each aligned block of 448 hidden units no cluster holds more than 28 units, and some cluster holds exactly 28; every cluster holds some unit.
All inputs are finite; a program needn't handle non-finite values.
Results may differ from a plain program's by a relative error of at most 0.023.
Values may be sent and summed in bfloat16 or wider, within the bound.
No kernel may reach another device: no remote copies, remote signals or barrier semaphores. Data moves between devices by JAX's collectives and lax.ppermute only.
A program may use at most 64 MiB of HBM per device.

v0:
```python
import jax
import jax.numpy as jnp
from jax import lax
from jax.sharding import PartitionSpec as P


def place_rows(labels, bin_count, capacity):
    count_rows = labels.shape[0]
    onehot = (labels[:, None] == jnp.arange(bin_count, dtype=jnp.int32)[None, :]).astype(jnp.int32)
    before = jnp.cumsum(onehot, axis=0) - onehot
    rank_in = jnp.sum(before * onehot, axis=1)
    position = labels * capacity + rank_in
    slot_list = jnp.full((bin_count * capacity,), count_rows, jnp.int32)
    slot_list = slot_list.at[position].set(jnp.arange(count_rows, dtype=jnp.int32))
    return (slot_list, position)


def with_zero_row(matrix):
    pad = jnp.zeros((1,) + matrix.shape[1:], matrix.dtype)
    return jnp.concatenate([matrix, pad], axis=0)


def against(left_side, right_side):
    return lax.dot_general(
        left_side, right_side, (((1,), (1,)), ((), ())), preferred_element_type=jnp.float32
    )


def on_device(tokens, router_weight, gate_weight, up_weight, down_weight, cluster_of, expert_ids):
    owners = lax.axis_size("dp")
    tensor_count = lax.axis_size("tensor")
    width_part = tokens.shape[1] // tensor_count
    token_count = tokens.shape[0]
    logits = jnp.dot(tokens, router_weight, preferred_element_type=jnp.float32)
    scores = jax.nn.sigmoid(jnp.take_along_axis(logits, expert_ids, axis=1))
    mixing = scores / jnp.sum(scores, axis=1, keepdims=True)
    stacked = jnp.stack([gate_weight, up_weight, down_weight], axis=1)
    rows = lax.all_to_all(stacked, "tensor", split_axis=2, concat_axis=0, tiled=True)
    unit_cap = 2 * rows.shape[0] // owners
    unit_list, unit_spot = place_rows(cluster_of[:, 0], owners, unit_cap)
    pick = with_zero_row(rows)[unit_list]
    own = lax.all_to_all(pick, "dp", split_axis=0, concat_axis=0, tiled=True)
    capacity = 4 * token_count // owners
    flat_ids = expert_ids.reshape(-1)
    slot_list, slot_spot = place_rows(flat_ids, owners, capacity)
    features = lax.dynamic_slice_in_dim(
        tokens, lax.axis_index("tensor") * width_part, width_part, 1
    )
    outgoing = with_zero_row(features)[slot_list // 2]
    arrived = lax.all_to_all(outgoing, "dp", split_axis=0, concat_axis=0, tiled=True)
    gate_part = against(arrived, own[:, 0, :]).astype(jnp.bfloat16)
    up_part = against(arrived, own[:, 1, :]).astype(jnp.bfloat16)
    both = jnp.stack([gate_part, up_part], axis=1)
    summed = lax.psum_scatter(both, "tensor", scatter_dimension=0, tiled=True).astype(jnp.float32)
    hidden_part = (jax.nn.silu(summed[:, 0, :]) * summed[:, 1, :]).astype(jnp.bfloat16)
    hidden = lax.all_gather(hidden_part, "tensor", axis=0, tiled=True)
    expert_out = jnp.dot(hidden, own[:, 2, :], preferred_element_type=jnp.float32).astype(
        jnp.bfloat16
    )
    returned = lax.all_to_all(expert_out, "dp", split_axis=0, concat_axis=0, tiled=True)
    picked_out = returned[slot_spot].reshape(token_count, 2, width_part)
    mixed_out = jnp.sum(mixing[:, :, None] * picked_out.astype(jnp.float32), axis=1)
    return mixed_out.astype(jnp.bfloat16)


def solution(mesh):
    in_specs = (
        P("dp", None),
        P(),
        P(("dp", "tensor"), None),
        P(("dp", "tensor"), None),
        P(("dp", "tensor"), None),
        P("dp", None),
        P("dp", None),
    )
    out_specs = P("dp", "tensor")
    return jax.shard_map(
        on_device, mesh=mesh, in_specs=in_specs, out_specs=out_specs, check_vma=False
    )
```

profile of v0, /device:TPU:1, one launch (start us, length us, event | category | flops | bytes accessed | tf_op | source)
XLA Modules:
  0.0 451.2 jit_solution(5226104023529939072)
XLA Ops:
  8.6 8.4 %copy.72 = bf16[56,3,8192]{0,1,2:T(4,128)(2,1)} copy(bf16[56,3,8192]{2,0,1:T(8,128)(2,1)S(1)} %pad_maximum_fusion.1) | data formatting | bytes 5505024 | tf_op jit(solution)/shard_map/stack | solution.py:37
  17.0 12.4 %reshape.154 = bf16[8,2,86016]{2,1,0:T(2,128)(2,1)} reshape(bf16[8192,3,56]{2,1,0:T(4,128)(2,1)} %bitcast.87) | data formatting | bytes 5505024
  29.4 9.1 %all-to-all-start.1 = ((bf16[8,2,86016]{2,1,0:T(2,128)(2,1)}), bf16[8,2,86016]{2,1,0:T(2,128)(2,1)S(1)}, u32[]{:S(2)}, u32[]{:S(2)}) async-start(bf16[8,2,86016]{2,1,0:T(2,128)(2,1)} %reshape.154), calls=%async_computation.1 | async-start | bytes 5505024 | tf_op jit(solution)/shard_map/all_to_all | solution.py:38
  40.2 2.9 scatter_custom_fusion.1
  43.1 61.2 %all-to-all-done.1 = bf16[8,2,86016]{2,1,0:T(2,128)(2,1)S(1)} async-done(((bf16[8,2,86016]{2,1,0:T(2,128)(2,1)}), bf16[8,2,86016]{2,1,0:T(2,128)(2,1)S(1)}, u32[]{:S(2)}, u32[]{:S(2)}) %all-to-all-start.1) | async-done | bytes 2752544 | tf_op jit(solution)/shard_map/all_to_all | solution.py:38
  104.3 13.2 %reshape.155 = bf16[8192,3,56]{2,1,0:T(4,128)(2,1)} reshape(bf16[8,2,86016]{2,1,0:T(2,128)(2,1)S(1)} %all-to-all-done.1) | data formatting | bytes 5505024
  117.5 10.6 %copy.79 = bf16[56,3,8,1024]{3,0,2,1:T(8,128)(2,1)S(1)} copy(bf16[56,3,8,1024]{0,1,3,2:T(4,128)(2,1)} %bitcast.88) | data formatting | bytes 5505024 | tf_op jit(solution)/shard_map/all_to_all | solution.py:38
  130.5 3.2 concatenate.7
  133.7 33.1 %gather_fusion.1 = bf16[896,3,1024]{2,1,0:T(4,128)(2,1)} fusion(bf16[449,3,1024]{2,1,0:T(4,128)(2,1)} %concatenate.7, s32[1024]{0:T(1024)S(1)} %pad_clamp_fusion.1), kind=kCustom, calls=%fused_computation.1 | custom fusion | bytes 11013632 | tf_op jit(solution)/shard_map/gather | solution.py:41
  166.8 7.6 %all-to-all-start.2 = ((bf16[896,3,1024]{2,1,0:T(4,128)(2,1)}), bf16[896,3,1024]{2,1,0:T(4,128)(2,1)}, u32[]{:S(2)}, u32[]{:S(2)}) async-start(bf16[896,3,1024]{2,1,0:T(4,128)(2,1)} %gather_fusion.1), calls=%async_computation.2 | async-start | bytes 14680064 | tf_op jit(solution)/shard_map/all_to_all | solution.py:42
  180.4 5.4 %gather_fusion = bf16[1024,1024]{1,0:T(8,128)(2,1)} fusion(bf16[257,1024]{1,0:T(8,128)(2,1)S(1)} %concatenate.6, s32[1024]{0:T(1024)S(1)} %fusion.21), kind=kCustom, calls=%fused_computation | custom fusion | bytes 4198400 | tf_op jit(solution)/shard_map/gather | solution.py:49
  185.7 75.9 %all-to-all-done.2 = bf16[896,3,1024]{2,1,0:T(4,128)(2,1)} async-done(((bf16[896,3,1024]{2,1,0:T(4,128)(2,1)}), bf16[896,3,1024]{2,1,0:T(4,128)(2,1)}, u32[]{:S(2)}, u32[]{:S(2)}) %all-to-all-start.2) | async-done | bytes 5505056 | tf_op jit(solution)/shard_map/all_to_all | solution.py:42
  261.6 8.7 %all-to-all-start = ((bf16[32,32,1024]{2,1,0:T(8,128)(2,1)}), bf16[32,32,1024]{2,1,0:T(8,128)(2,1)S(1)}, u32[]{:S(2)}, u32[]{:S(2)}) async-start(bf16[32,32,1024]{2,1,0:T(8,128)(2,1)} %bitcast.4), calls=%async_computation | async-start | bytes 4194304 | tf_op jit(solution)/shard_map/all_to_all | solution.py:50
  270.4 18.2 %fusion.28 = (bf16[896,1,1024]{2,1,0:T(2,128)(2,1)}, bf16[896,1,1024]{2,1,0:T(2,128)(2,1)}, bf16[896,1,1024]{2,1,0:T(2,128)(2,1)}) fusion(bf16[896,3,1024]{2,1,0:T(4,128)(2,1)} %all-to-all-done.2), kind=kLoop, calls=%fused_computation.70 | loop fusion | bytes 11010048 | tf_op jit(solution)/shard_map/slice | solution.py:57
  288.6 10.0 %all-to-all-done = bf16[32,32,1024]{2,1,0:T(8,128)(2,1)S(1)} async-done(((bf16[32,32,1024]{2,1,0:T(8,128)(2,1)}), bf16[32,32,1024]{2,1,0:T(8,128)(2,1)S(1)}, u32[]{:S(2)}, u32[]{:S(2)}) %all-to-all-start) | async-done | bytes 2097184 | tf_op jit(solution)/shard_map/all_to_all | solution.py:50
  298.6 4.6 %convert_bitcast_fusion.1 = bf16[1024,1,896]{2,0,1:T(8,128)(2,1)S(1)} fusion(bf16[1024,1024]{1,0:T(8,128)(2,1)S(1)} %bitcast.91, bf16[896,1,1024]{2,1,0:T(2,128)(2,1)} %get-tuple-element.9), kind=kOutput, calls=%fused_computation.19 | convolution fusion | flops 1879965696 | bytes 5767168 | tf_op jit(solution)/shard_map/dot_general | solution.py:24
  307.9 44.0 %reduce-scatter.2.cloned.1.call-done = bf16[128,2,896]{2,0,1:T(8,128)(2,1)} async-done(((bf16[1024,2,896]{2,0,1:T(8,128)(2,1)}), bf16[128,2,896]{2,0,1:T(8,128)(2,1)}) %reduce-scatter.2.cloned.1.call-update) | async-done | bytes 458768 | tf_op jit(solution)/shard_map/reduce_scatter | solution.py:54
  353.8 35.5 %all-gather.2.cloned.1.call-done = bf16[1024,896]{1,0:T(8,128)(2,1)} async-done(((bf16[128,896]{1,0:T(8,128)(2,1)}), bf16[1024,896]{1,0:T(8,128)(2,1)}) %all-gather.2.cloned.1.call-update) | async-done | bytes 1835024 | tf_op jit(solution)/shard_map/all_gather | solution.py:56
  389.3 6.3 %convolution_convert_fusion = bf16[1024,1024]{1,0:T(8,128)(2,1)} fusion(bf16[1024,896]{1,0:T(8,128)(2,1)} %all-gather.2.cloned.1.call-done, bf16[896,1,1024]{2,1,0:T(2,128)(2,1)} %get-tuple-element.7), kind=kOutput, calls=%fused_computation.9 | convolution fusion | flops 1880096768 | bytes 5767168 | tf_op jit(solution)/shard_map/dot_general | solution.py:57
  395.6 11.6 %all-to-all-start.3 = ((bf16[32,32,1024]{2,1,0:T(8,128)(2,1)}), bf16[32,32,1024]{2,1,0:T(8,128)(2,1)S(1)}, u32[]{:S(2)}, u32[]{:S(2)}) async-start(bf16[32,32,1024]{2,1,0:T(8,128)(2,1)} %bitcast.90), calls=%async_computation.4 | async-start | bytes 4194304 | tf_op jit(solution)/shard_map/all_to_all | solution.py:60
  407.5 3.5 fusion.29
  411.1 4.5 %gather_fusion.3 = f32[512]{0:T(512)S(1)} fusion(f32[256,32]{0,1:T(8,128)S(1)} %fusion.29, s32[512]{0:T(512)S(1)} %reshape.119), kind=kCustom, calls=%fused_computation.3 | custom fusion | bytes 8192 | tf_op jit(solution)/shard_map/jit(take_along_axis)/gather | solution.py:35
  416.1 19.6 %all-to-all-done.3 = bf16[32,32,1024]{2,1,0:T(8,128)(2,1)S(1)} async-done(((bf16[32,32,1024]{2,1,0:T(8,128)(2,1)}), bf16[32,32,1024]{2,1,0:T(8,128)(2,1)S(1)}, u32[]{:S(2)}, u32[]{:S(2)}) %all-to-all-start.3) | async-done | bytes 2097184 | tf_op jit(solution)/shard_map/all_to_all | solution.py:60
  440.9 3.5 multiply_reduce_fusion
  (61 shorter events, 24.3 us)
Async XLA Ops:
  6.5 401.0 %copy-start = (bf16[8192,32]{0,1:T(8,128)(2,1)S(1)}, bf16[8192,32]{0,1:T(8,128)(2,1)}, u32[]{:S(2)}) copy-start(bf16[8192,32]{0,1:T(8,128)(2,1)} %param.8) | copy-start | bytes 1572868
  29.4 9.1 %copy-start.4 = (s32[448,1]{0,1:T(1,128)S(1)}, s32[448,1]{0,1:T(1,128)}, u32[]{:S(2)}) copy-start(s32[448,1]{0,1:T(1,128)} %param.12) | copy-start | bytes 5380
  29.4 74.9 %all-to-all-start.1 = ((bf16[8,2,86016]{2,1,0:T(2,128)(2,1)}), bf16[8,2,86016]{2,1,0:T(2,128)(2,1)S(1)}, u32[]{:S(2)}, u32[]{:S(2)}) async-start(bf16[8,2,86016]{2,1,0:T(2,128)(2,1)} %reshape.154), calls=%async_computation.1 | async-start | bytes 5505024 | tf_op jit(solution)/shard_map/all_to_all | solution.py:38
  166.8 7.7 %copy-start.3 = (s32[256,2]{0,1:T(2,128)S(1)}, s32[256,2]{0,1:T(2,128)}, u32[]{:S(2)}) copy-start(s32[256,2]{0,1:T(2,128)} %param.13) | copy-start | bytes 6148
  166.8 94.8 %all-to-all-start.2 = ((bf16[896,3,1024]{2,1,0:T(4,128)(2,1)}), bf16[896,3,1024]{2,1,0:T(4,128)(2,1)}, u32[]{:S(2)}, u32[]{:S(2)}) async-start(bf16[896,3,1024]{2,1,0:T(4,128)(2,1)} %gather_fusion.1), calls=%async_computation.2 | async-start | bytes 14680064 | tf_op jit(solution)/shard_map/all_to_all | solution.py:42
  261.6 37.0 %all-to-all-start = ((bf16[32,32,1024]{2,1,0:T(8,128)(2,1)}), bf16[32,32,1024]{2,1,0:T(8,128)(2,1)S(1)}, u32[]{:S(2)}, u32[]{:S(2)}) async-start(bf16[32,32,1024]{2,1,0:T(8,128)(2,1)} %bitcast.4), calls=%async_computation | async-start | bytes 4194304 | tf_op jit(solution)/shard_map/all_to_all | solution.py:50
  270.3 81.6 %reduce-scatter.2.cloned.1.call-start = ((), (), s32[]{:S(2)}) async-start(), calls=%async_computation.5 | async-start | bytes 4128768 | tf_op jit(solution)/shard_map/reduce_scatter | solution.py:54
  298.6 4.6 %copy-start.2 = (bf16[896,1,1024]{2,1,0:T(2,128)(2,1)S(1)}, bf16[896,1,1024]{2,1,0:T(2,128)(2,1)}, u32[]{:S(2)}) copy-start(bf16[896,1,1024]{2,1,0:T(2,128)(2,1)} %get-tuple-element.8) | copy-start | bytes 5505028
  307.8 81.5 %all-gather.2.cloned.1.call-start = ((), (), s32[]{:S(2)}) async-start(), calls=%async_computation.6 | async-start | bytes 2064384 | tf_op jit(solution)/shard_map/all_gather | solution.py:56
  395.6 40.1 %all-to-all-start.3 = ((bf16[32,32,1024]{2,1,0:T(8,128)(2,1)}), bf16[32,32,1024]{2,1,0:T(8,128)(2,1)S(1)}, u32[]{:S(2)}, u32[]{:S(2)}) async-start(bf16[32,32,1024]{2,1,0:T(8,128)(2,1)} %bitcast.90), calls=%async_computation.4 | async-start | bytes 4194304 | tf_op jit(solution)/shard_map/all_to_all | solution.py:60
  435.7 8.6 %copy-start.1 = (bf16[8192,32]{0,1:T(8,128)(2,1)S(1)}, bf16[8192,32]{0,1:T(8,128)(2,1)}, u32[]{:S(2)}) copy-start(bf16[8192,32]{0,1:T(8,128)(2,1)} %param.8) | copy-start | bytes 1572868
Sparse Core Ops, SparseCore 0:
  307.9 43.9 reduce-scatter.1
  353.9 35.3 all-gather.1
where the time goes:
time: 452 us; the launch traced here: 451 us
  waiting for transfers between devices  246 us (54%)
  local copies, waits for them, and re-layouts  125 us (28%)
  starting transfers between devices  37.2 us (8%)
  matrix products  16.8 us (4%)
  between operations  13.8 us (3%)
  other arithmetic  12.4 us (3%)
    all_to_all x1, waiting for transfers between devices, on_device(): own = lax.all_to_all(pick, 'dp', split_axis=0, concat_axis=0, tiled=True)  75.9 us
    all_to_all x1, waiting for transfers between devices, on_device(): lax.all_to_all(stacked, 'tensor', split_axis=2, concat_axis=0, tiled=True)  61.2 us
    reduce_scatter x1, waiting for transfers between devices, on_device(): lax.psum_scatter(both, 'tensor', scatter_dimension=0, tiled=True)  44 us
    all_gather x1, waiting for transfers between devices, on_device(): hidden = lax.all_gather(hidden_part, 'tensor', axis=0, tiled=True)  35.5 us
    gather x1, local copies, waits for them, and re-layouts, on_device(): pick = with_zero_row(rows)[unit_list]  33.1 us
    unnamed x13, local copies, waits for them, and re-layouts  25.7 us
    all_to_all x1, waiting for transfers between devices, on_device(): lax.all_to_all(expert_out, 'dp', split_axis=0, concat_axis=0, tiled=True)  19.6 us
    slice x1, local copies, waits for them, and re-layouts, on_device(): own[:, 2, :]  18.2 us
  transfers between devices with their start and end apart: 6, of which 6 were waited for; matrix products, arithmetic and copies ran while one was open for 9% of the time, Pallas kernels for 0%

commit v1 on v0

--- a/solution.py
+++ b/solution.py
@@ -35,7 +35,12 @@
     scores = jax.nn.sigmoid(jnp.take_along_axis(logits, expert_ids, axis=1))
     mixing = scores / jnp.sum(scores, axis=1, keepdims=True)
     stacked = jnp.stack([gate_weight, up_weight, down_weight], axis=1)
-    rows = lax.all_to_all(stacked, "tensor", split_axis=2, concat_axis=0, tiled=True)
+    rows = jnp.concatenate(
+        lax.all_to_all(
+            jnp.stack(jnp.split(stacked, lax.axis_size("tensor"), axis=2)), "tensor", 0, 0
+        ),
+        axis=0,
+    )
     unit_cap = 2 * rows.shape[0] // owners
     unit_list, unit_spot = place_rows(cluster_of[:, 0], owners, unit_cap)
     pick = with_zero_row(rows)[unit_list]

time: 452 us -> 414 us (0.916)
  local copies, waits for them, and re-layouts: 125 us -> 86.7 us
    unnamed x13 -> x18, local copies, waits for them, and re-layouts: 25.7 us -> 5.52 us
    all_to_all x2 -> x1, local copies, waits for them, and re-layouts: 13 us -> 0.28 us  [on_device(): lax.all_to_all(jnp.stack(jnp.split(stacked, lax.axis_size('tensor'), axis...]
    another operation x4, local copies, waits for them, and re-layouts: 8.63 us -> 0.99 us  [the longest x1 0.76 us: on_device(): jnp.stack(jnp.split(stacked, lax.axis_size('tensor'), axis=2))]
    all_to_all x1, waiting for transfers between devices: 75.9 us -> 80.6 us  [on_device(): own = lax.all_to_all(pick, 'dp', split_axis=0, concat_axis=0, tiled=True)]
    all_to_all x1, waiting for transfers between devices: 61.2 us -> 56.4 us  [on_device(): lax.all_to_all(jnp.stack(jnp.split(stacked, lax.axis_size('tensor'), axis...]
  transfers between devices with their start and end apart: 6 -> 6, of which waited for: 6 -> 6; matrix products, arithmetic and copies ran while one was open for 9% -> 10% of each run, Pallas kernels for 0% -> 0%
where the time goes in v1:
time: 414 us; the launch traced here: 413 us
  waiting for transfers between devices  246 us (59%)
  local copies, waits for them, and re-layouts  86.7 us (21%)
  starting transfers between devices  37.2 us (9%)
  matrix products  16.8 us (4%)
  between operations  13.7 us (3%)
  other arithmetic  12.4 us (3%)
    all_to_all x1, waiting for transfers between devices, on_device(): own = lax.all_to_all(pick, 'dp', split_axis=0, concat_axis=0, tiled=True)  80.6 us
    all_to_all x1, waiting for transfers between devices, on_device(): lax.all_to_all(jnp.stack(jnp.split(stacked, lax.axis_size('tensor'), axis...  56.4 us
    reduce_scatter x1, waiting for transfers between devices, on_device(): lax.psum_scatter(both, 'tensor', scatter_dimension=0, tiled=True)  44 us
    all_gather x1, waiting for transfers between devices, on_device(): hidden = lax.all_gather(hidden_part, 'tensor', axis=0, tiled=True)  35.5 us
    gather x1, local copies, waits for them, and re-layouts, on_device(): pick = with_zero_row(rows)[unit_list]  33.1 us
    all_to_all x1, waiting for transfers between devices, on_device(): lax.all_to_all(expert_out, 'dp', split_axis=0, concat_axis=0, tiled=True)  19.6 us
    slice x1, local copies, waits for them, and re-layouts, on_device(): own[:, 2, :]  18.2 us
    all_to_all x1, starting transfers between devices, on_device(): lax.all_to_all(expert_out, 'dp', split_axis=0, concat_axis=0, tiled=True)  11.6 us
  transfers between devices with their start and end apart: 6, of which 6 were waited for; matrix products, arithmetic and copies ran while one was open for 10% of the time, Pallas kernels for 0%

profile of v1, /device:TPU:1, one launch (start us, length us, event | category | flops | bytes accessed | tf_op | source)
XLA Modules:
  0.0 413.1 jit_solution(13415604123316097258)
XLA Ops:
  14.8 9.1 %all-to-all-start.1 = ((bf16[8,56,3,1024]{3,1,2,0:T(8,128)(2,1)}), bf16[8,56,3,1024]{3,1,2,0:T(8,128)(2,1)S(1)}, u32[]{:S(2)}, u32[]{:S(2)}) async-start(bf16[8,56,3,1024]{3,1,2,0:T(8,128)(2,1)} %fusion.14), calls=%async_computation.1 | async-start | bytes 5505024 | tf_op jit(solution)/shard_map/all_to_all | solution.py:39
  27.7 2.4 scatter_custom_fusion
  30.3 2.9 scatter_custom_fusion.1
  33.2 56.4 %all-to-all-done.1 = bf16[8,56,3,1024]{3,1,2,0:T(8,128)(2,1)S(1)} async-done(((bf16[8,56,3,1024]{3,1,2,0:T(8,128)(2,1)}), bf16[8,56,3,1024]{3,1,2,0:T(8,128)(2,1)S(1)}, u32[]{:S(2)}, u32[]{:S(2)}) %all-to-all-start.1) | async-done | bytes 2752544 | tf_op jit(solution)/shard_map/all_to_all | solution.py:39
  92.3 3.2 concatenate.7
  95.5 33.1 %gather_fusion.1 = bf16[896,3,1024]{2,1,0:T(4,128)(2,1)} fusion(bf16[449,3,1024]{2,1,0:T(4,128)(2,1)} %concatenate.7, s32[1024]{0:T(1024)S(1)} %get-tuple-element.11), kind=kCustom, calls=%fused_computation.1 | custom fusion | bytes 11013632 | tf_op jit(solution)/shard_map/gather | solution.py:46
  128.6 7.6 %all-to-all-start.2 = ((bf16[896,3,1024]{2,1,0:T(4,128)(2,1)}), bf16[896,3,1024]{2,1,0:T(4,128)(2,1)}, u32[]{:S(2)}, u32[]{:S(2)}) async-start(bf16[896,3,1024]{2,1,0:T(4,128)(2,1)} %gather_fusion.1), calls=%async_computation.2 | async-start | bytes 14680064 | tf_op jit(solution)/shard_map/all_to_all | solution.py:47
  137.4 5.4 %gather_fusion = bf16[1024,1024]{1,0:T(8,128)(2,1)} fusion(bf16[257,1024]{1,0:T(8,128)(2,1)S(1)} %concatenate.6, s32[1024]{0:T(1024)S(1)} %get-tuple-element.10), kind=kCustom, calls=%fused_computation | custom fusion | bytes 4198400 | tf_op jit(solution)/shard_map/gather | solution.py:54
  142.8 80.6 %all-to-all-done.2 = bf16[896,3,1024]{2,1,0:T(4,128)(2,1)} async-done(((bf16[896,3,1024]{2,1,0:T(4,128)(2,1)}), bf16[896,3,1024]{2,1,0:T(4,128)(2,1)}, u32[]{:S(2)}, u32[]{:S(2)}) %all-to-all-start.2) | async-done | bytes 5505056 | tf_op jit(solution)/shard_map/all_to_all | solution.py:47
  223.4 8.7 %all-to-all-start = ((bf16[32,32,1024]{2,1,0:T(8,128)(2,1)}), bf16[32,32,1024]{2,1,0:T(8,128)(2,1)S(1)}, u32[]{:S(2)}, u32[]{:S(2)}) async-start(bf16[32,32,1024]{2,1,0:T(8,128)(2,1)} %bitcast.4), calls=%async_computation | async-start | bytes 4194304 | tf_op jit(solution)/shard_map/all_to_all | solution.py:55
  232.2 18.2 %fusion.36 = (bf16[896,1,1024]{2,1,0:T(2,128)(2,1)}, bf16[896,1,1024]{2,1,0:T(2,128)(2,1)}, bf16[896,1,1024]{2,1,0:T(2,128)(2,1)}) fusion(bf16[896,3,1024]{2,1,0:T(4,128)(2,1)} %all-to-all-done.2), kind=kLoop, calls=%fused_computation.86 | loop fusion | bytes 11010048 | tf_op jit(solution)/shard_map/slice | solution.py:62
  250.5 10.0 %all-to-all-done = bf16[32,32,1024]{2,1,0:T(8,128)(2,1)S(1)} async-done(((bf16[32,32,1024]{2,1,0:T(8,128)(2,1)}), bf16[32,32,1024]{2,1,0:T(8,128)(2,1)S(1)}, u32[]{:S(2)}, u32[]{:S(2)}) %all-to-all-start) | async-done | bytes 2097184 | tf_op jit(solution)/shard_map/all_to_all | solution.py:55
  260.5 4.6 %convert_bitcast_fusion.1 = bf16[1024,1,896]{2,0,1:T(8,128)(2,1)S(1)} fusion(bf16[1024,1024]{1,0:T(8,128)(2,1)S(1)} %bitcast.115, bf16[896,1,1024]{2,1,0:T(2,128)(2,1)} %get-tuple-element.9), kind=kOutput, calls=%fused_computation.19 | convolution fusion | flops 1879965696 | bytes 5767168 | tf_op jit(solution)/shard_map/dot_general | solution.py:24
  265.1 2.4 convert_bitcast_fusion
  269.7 44.0 %reduce-scatter.2.cloned.1.call-done = bf16[128,2,896]{2,0,1:T(8,128)(2,1)} async-done(((bf16[1024,2,896]{2,0,1:T(8,128)(2,1)}), bf16[128,2,896]{2,0,1:T(8,128)(2,1)}) %reduce-scatter.2.cloned.1.call-update) | async-done | bytes 458768 | tf_op jit(solution)/shard_map/reduce_scatter | solution.py:59
  315.6 35.5 %all-gather.2.cloned.1.call-done = bf16[1024,896]{1,0:T(8,128)(2,1)} async-done(((bf16[128,896]{1,0:T(8,128)(2,1)}), bf16[1024,896]{1,0:T(8,128)(2,1)}) %all-gather.2.cloned.1.call-update) | async-done | bytes 1835024 | tf_op jit(solution)/shard_map/all_gather | solution.py:61
  351.1 6.3 %convolution_convert_fusion = bf16[1024,1024]{1,0:T(8,128)(2,1)} fusion(bf16[1024,896]{1,0:T(8,128)(2,1)} %all-gather.2.cloned.1.call-done, bf16[896,1,1024]{2,1,0:T(2,128)(2,1)} %get-tuple-element.7), kind=kOutput, calls=%fused_computation.9 | convolution fusion | flops 1880096768 | bytes 5767168 | tf_op jit(solution)/shard_map/dot_general | solution.py:62
  357.4 11.6 %all-to-all-start.3 = ((bf16[32,32,1024]{2,1,0:T(8,128)(2,1)}), bf16[32,32,1024]{2,1,0:T(8,128)(2,1)S(1)}, u32[]{:S(2)}, u32[]{:S(2)}) async-start(bf16[32,32,1024]{2,1,0:T(8,128)(2,1)} %bitcast.114), calls=%async_computation.4 | async-start | bytes 4194304 | tf_op jit(solution)/shard_map/all_to_all | solution.py:65
  369.4 3.5 fusion.37
  372.9 4.5 %gather_fusion.3 = f32[512]{0:T(512)S(1)} fusion(f32[256,32]{0,1:T(8,128)S(1)} %fusion.37, s32[512]{0:T(512)S(1)} %reshape.123), kind=kCustom, calls=%fused_computation.3 | custom fusion | bytes 8192 | tf_op jit(solution)/shard_map/jit(take_along_axis)/gather | solution.py:35
  377.9 19.6 %all-to-all-done.3 = bf16[32,32,1024]{2,1,0:T(8,128)(2,1)S(1)} async-done(((bf16[32,32,1024]{2,1,0:T(8,128)(2,1)}), bf16[32,32,1024]{2,1,0:T(8,128)(2,1)S(1)}, u32[]{:S(2)}, u32[]{:S(2)}) %all-to-all-start.3) | async-done | bytes 2097184 | tf_op jit(solution)/shard_map/all_to_all | solution.py:65
  397.6 2.8 gather_fusion.2
  400.4 2.4 reshape.98
  402.7 3.5 multiply_reduce_fusion
  (65 shorter events, 20.7 us)
Async XLA Ops:
  6.5 362.8 %copy-start = (bf16[8192,32]{0,1:T(8,128)(2,1)S(1)}, bf16[8192,32]{0,1:T(8,128)(2,1)}, u32[]{:S(2)}) copy-start(bf16[8192,32]{0,1:T(8,128)(2,1)} %param.8) | copy-start | bytes 1572868
  14.8 9.1 %copy-start.3 = (s32[256,2]{0,1:T(2,128)S(1)}, s32[256,2]{0,1:T(2,128)}, u32[]{:S(2)}) copy-start(s32[256,2]{0,1:T(2,128)} %param.13) | copy-start | bytes 6148
  14.8 11.3 %copy-start.4 = (s32[448,1]{0,1:T(1,128)S(1)}, s32[448,1]{0,1:T(1,128)}, u32[]{:S(2)}) copy-start(s32[448,1]{0,1:T(1,128)} %param.12) | copy-start | bytes 5380
  14.8 74.9 %all-to-all-start.1 = ((bf16[8,56,3,1024]{3,1,2,0:T(8,128)(2,1)}), bf16[8,56,3,1024]{3,1,2,0:T(8,128)(2,1)S(1)}, u32[]{:S(2)}, u32[]{:S(2)}) async-start(bf16[8,56,3,1024]{3,1,2,0:T(8,128)(2,1)} %fusion.14), calls=%async_computation.1 | async-start | bytes 5505024 | tf_op jit(solution)/shard_map/all_to_all | solution.py:39
  128.6 94.8 %all-to-all-start.2 = ((bf16[896,3,1024]{2,1,0:T(4,128)(2,1)}), bf16[896,3,1024]{2,1,0:T(4,128)(2,1)}, u32[]{:S(2)}, u32[]{:S(2)}) async-start(bf16[896,3,1024]{2,1,0:T(4,128)(2,1)} %gather_fusion.1), calls=%async_computation.2 | async-start | bytes 14680064 | tf_op jit(solution)/shard_map/all_to_all | solution.py:47
  223.4 37.0 %all-to-all-start = ((bf16[32,32,1024]{2,1,0:T(8,128)(2,1)}), bf16[32,32,1024]{2,1,0:T(8,128)(2,1)S(1)}, u32[]{:S(2)}, u32[]{:S(2)}) async-start(bf16[32,32,1024]{2,1,0:T(8,128)(2,1)} %bitcast.4), calls=%async_computation | async-start | bytes 4194304 | tf_op jit(solution)/shard_map/all_to_all | solution.py:55
  232.2 81.6 %reduce-scatter.2.cloned.1.call-start = ((), (), s32[]{:S(2)}) async-start(), calls=%async_computation.5 | async-start | bytes 4128768 | tf_op jit(solution)/shard_map/reduce_scatter | solution.py:59
  260.5 4.6 %copy-start.2 = (bf16[896,1,1024]{2,1,0:T(2,128)(2,1)S(1)}, bf16[896,1,1024]{2,1,0:T(2,128)(2,1)}, u32[]{:S(2)}) copy-start(bf16[896,1,1024]{2,1,0:T(2,128)(2,1)} %get-tuple-element.8) | copy-start | bytes 5505028
  269.6 81.5 %all-gather.2.cloned.1.call-start = ((), (), s32[]{:S(2)}) async-start(), calls=%async_computation.6 | async-start | bytes 2064384 | tf_op jit(solution)/shard_map/all_gather | solution.py:61
  357.4 40.1 %all-to-all-start.3 = ((bf16[32,32,1024]{2,1,0:T(8,128)(2,1)}), bf16[32,32,1024]{2,1,0:T(8,128)(2,1)S(1)}, u32[]{:S(2)}, u32[]{:S(2)}) async-start(bf16[32,32,1024]{2,1,0:T(8,128)(2,1)} %bitcast.114), calls=%async_computation.4 | async-start | bytes 4194304 | tf_op jit(solution)/shard_map/all_to_all | solution.py:65
  397.6 8.6 %copy-start.1 = (bf16[8192,32]{0,1:T(8,128)(2,1)S(1)}, bf16[8192,32]{0,1:T(8,128)(2,1)}, u32[]{:S(2)}) copy-start(bf16[8192,32]{0,1:T(8,128)(2,1)} %param.8) | copy-start | bytes 1572868
Sparse Core Ops, SparseCore 0:
  269.8 43.9 reduce-scatter.1
  315.8 35.3 all-gather.1
